TPU v7x, 32 devices: a whole 2x2x4 slice. The times are simulated.
32 devices in a mesh: dp: 16 (over z, y, core), tensor: 2 (over x).
Axes of the slice: x: 2, y: 2, z: 4, core: 2. Of those that a mesh axis runs over, the one named last changes fastest.
Arguments:
- hidden_states: bfloat16 [8192, 2048], P('dp', 'tensor'), may hold values from -6 to 6
- norm_gain: bfloat16 [2048], replicated, may hold values from 0.25 to 1.75
- head_weight: bfloat16 [2048, 25600], P(None, ('tensor', 'dp')), may hold values from -1 to 1
- target_ids: int32 [8192], P('dp'), may hold values from 0 to 25599
- loss_mask: int32 [8192], P('dp'), may hold values from 0 to 1, as said below
- seq_lengths: int32 [16], replicated, may hold values from 1 to 4096, as said below
- slot_order: int32 [16], replicated, may hold values from 0 to 15, each once
Outputs:
- token_logprob: float32 [8192], P(('dp', 'tensor'))
- token_entropy: float32 [8192], P(('dp', 'tensor'))
- seq_mean_logprob: float32 [16], P('dp')
- seq_mean_entropy: float32 [16], P('dp')
Inputs may be any that keep to these rules, and one draw needn't show every extreme that they name: `seq_lengths`: sequences lie in packed order, one after another; their lengths sum to 8192; the longest has exactly 4096 tokens and some sequence has exactly 1 token. `slot_order`: each sequence appears once. `loss_mask`: some sequence of exactly 1 token has no scored row.
All inputs are finite; a program needn't handle non-finite values.
Results may differ from a plain program's by a relative error of at most 0.0012.
Values may be sent and summed in bfloat16 or wider, within the bound.
No kernel may reach another device: no remote copies, remote signals or barrier semaphores. Data moves between devices by JAX's collectives and lax.ppermute only.
A program may use at most 192 MiB of HBM per device.

v0:
```python
import jax
import jax.numpy as jnp
from jax import lax
from jax.sharding import PartitionSpec as P

EPS = 1e-05


def per_device(
    hidden_states, norm_gain, head_weight, target_ids, loss_mask, seq_lengths, slot_order
):
    whole = lax.all_gather(hidden_states, "tensor", axis=1, tiled=True)
    values = whole.astype(jnp.float32)
    square = jnp.mean(values * values, axis=1, keepdims=True)
    normed = (values * lax.rsqrt(square + EPS) * norm_gain.astype(jnp.float32)).astype(jnp.bfloat16)
    rows = whole.shape[0]
    groups = lax.axis_size("tensor")
    share = rows // groups
    column_base = lax.axis_index("tensor") * (head_weight.shape[1] * lax.axis_size("dp"))
    piece = lax.all_gather(head_weight, "dp", axis=1, tiled=True)
    top = jnp.full((rows,), -1e30, jnp.float32)
    total = jnp.zeros((rows,), jnp.float32)
    logits = jnp.dot(normed, piece, preferred_element_type=jnp.float32)
    columns = column_base + lax.broadcasted_iota(jnp.int32, (1, piece.shape[1]), 1)
    new_top = jnp.maximum(top, jnp.max(logits, axis=1))
    shifted = logits - new_top[:, None]
    expo = jnp.exp(shifted)
    scale = jnp.exp(top - new_top)
    new_total = jnp.sum(expo, axis=1)
    new_spread = scale * (total * (top - new_top)) + jnp.sum(expo * shifted, axis=1)
    hit = jnp.sum(jnp.where(columns == target_ids[:, None], logits, 0.0), axis=1)
    mine = lax.axis_index("tensor") * share
    row_top = lax.pmax(new_top, "tensor")
    scale = jnp.exp(new_top - row_top)
    sums = lax.psum(
        (new_total * scale, scale * (new_spread + new_total * (new_top - row_top)), hit), "tensor"
    )
    row_top = lax.dynamic_slice_in_dim(row_top, mine, share)
    row_total = lax.dynamic_slice_in_dim(sums[0], mine, share)
    row_spread = lax.dynamic_slice_in_dim(sums[1], mine, share)
    row_picked = lax.dynamic_slice_in_dim(sums[2], mine, share)
    logsum = jnp.log(row_total)
    live = lax.dynamic_slice_in_dim(loss_mask, mine, share).astype(jnp.float32)
    token_logprob = (row_picked - row_top - logsum) * live
    token_entropy = (logsum - row_spread / row_total) * live
    ends = jnp.cumsum(seq_lengths)
    position = lax.axis_index("dp") * rows + mine + jnp.arange(share, dtype=jnp.int32)
    segment = jnp.sum((position[:, None] >= ends[None, :]).astype(jnp.int32), axis=1)
    member = (segment[:, None] == slot_order[None, :]).astype(jnp.float32)
    lp_part = jnp.dot(token_logprob, member, precision=lax.Precision.HIGHEST)
    ent_part = jnp.dot(token_entropy, member, precision=lax.Precision.HIGHEST)
    count_part = jnp.dot(live, member, precision=lax.Precision.HIGHEST)
    lp_sum, ent_sum, count = lax.psum((lp_part, ent_part, count_part), ("dp", "tensor"))
    owned = lp_sum.shape[0] // lax.axis_size("dp")
    first_slot = lax.axis_index("dp") * owned
    floor = jnp.maximum(lax.dynamic_slice_in_dim(count, first_slot, owned), 1.0)
    seq_mean_logprob = lax.dynamic_slice_in_dim(lp_sum, first_slot, owned) / floor
    seq_mean_entropy = lax.dynamic_slice_in_dim(ent_sum, first_slot, owned) / floor
    return (token_logprob, token_entropy, seq_mean_logprob, seq_mean_entropy)


def solution(mesh):
    placed = (P("dp", "tensor"), P(), P(None, ("tensor", "dp")), P("dp"), P("dp"), P(), P())
    return jax.shard_map(
        per_device,
        mesh=mesh,
        in_specs=placed,
        out_specs=(P(("dp", "tensor")), P(("dp", "tensor")), P("dp"), P("dp")),
        check_vma=False,
    )
```

profile of v0, /device:TPU:0, one launch (start us, length us, event | category | flops | bytes accessed | tf_op | source)
XLA Modules:
  0.0 416.9 jit_solution(15467861116896965682)
XLA Ops:
  7.2 0.0 all-gather.3.cloned.1.call-start
  7.2 0.7 all-gather.3.cloned.1.call-update
  7.9 0.0 all-gather.5.cloned.1.call-start
  7.9 0.7 all-gather.5.cloned.1.call-update
  8.7 0.7 convert_element_type.17
  9.3 0.7 copy.13
  10.1 0.1 reduce
  10.2 0.1 convert_reduce_fusion
  10.3 35.1 %all-gather.3.cloned.1.call-done = bf16[512,2048]{1,0:T(8,128)(2,1)} async-done(((bf16[512,1024]{1,0:T(8,128)(2,1)}), bf16[512,2048]{1,0:T(8,128)(2,1)}) %all-gather.3.cloned.1.call-update) | async-done | bytes 2097168 | tf_op jit(solution)/shard_map/all_gather | solution.py:12
  45.4 2.1 fusion.1
  47.5 256.5 %all-gather.5.cloned.1.call-done = bf16[2048,12800]{0,1:T(8,128)(2,1)} async-done(((bf16[2048,800]{0,1:T(8,128)(2,1)}), bf16[2048,12800]{0,1:T(8,128)(2,1)}) %all-gather.5.cloned.1.call-update) | async-done | bytes 52428816 | tf_op jit(solution)/shard_map/all_gather | solution.py:20
  304.0 35.8 %fusion.17 = (f32[512]{0:T(512)S(1)}, f32[512,12800]{1,0:T(8,128)}) fusion(bf16[2048,12800]{0,1:T(8,128)(2,1)} %all-gather.5.cloned.1.call-done, bf16[512,2048]{1,0:T(8,128)(2,1)} %all-gather.3.cloned.1.call-done, f32[2048]{0:T(1024)S(1)} %convert_element_type.17, f32[512]{0:T(512)S(1)} %add_rsqrt_fusion), kind=kOutput, calls=%fused_computation.34 | convolution fusion | flops 26854293504 | bytes 80752640 | tf_op jit(solution)/shard_map/dot_general | solution.py:23
  339.9 4.9 %pmax.7 = f32[512]{0:T(512)S(1)} all-reduce(f32[512]{0:T(512)S(1)} %broadcast_maximum_fusion), channel_id=1, replica_groups=mesh['dp'=16,'tensor'=2] {'tensor'}, use_global_device_ids=true, to_apply=%region_4.5 | all-reduce | flops 512 | bytes 4096 | tf_op jit(solution)/shard_map/pmax | solution.py:33
  344.8 13.5 %fusion = (f32[512]{0:T(512)S(1)}, f32[512]{0:T(512)S(1)}, f32[512]{0:T(512)S(1)}) fusion(f32[512,12800]{1,0:T(8,128)} %get-tuple-element.18, f32[512]{0:T(512)S(1)} %broadcast_maximum_fusion, s32[512]{0:T(512)S(1)} %copy-done, s32[12800]{0:T(1024)S(1)} %iota_add_fusion), kind=kLoop, calls=%fused_computation.2 | loop fusion | flops 45873664 | bytes 26275840 | tf_op jit(solution)/shard_map/reduce_sum | solution.py:30
  358.3 5.0 %all-reduce.1 = (f32[512]{0:T(512)S(1)}, f32[512]{0:T(512)S(1)}, f32[512]{0:T(512)S(1)}) all-reduce(f32[512]{0:T(512)S(1)} %get-tuple-element.6, f32[512]{0:T(512)S(1)} %get-tuple-element.16, f32[512]{0:T(512)S(1)} %get-tuple-element.15), channel_id=1, replica_groups=mesh['dp'=16,'tensor'=2] {'tensor'}, use_global_device_ids=true, to_apply=%region_2.0 | all-reduce | flops 1536 | bytes 12288 | tf_op jit(solution)/shard_map/psum | solution.py:35
  363.3 0.1 subtract_multiply_fusion
  363.4 0.2 convolution_bitcast_fusion
  363.6 0.2 convolution_bitcast_fusion.1
  363.9 0.1 subtract_multiply_fusion.1
  364.0 0.2 convolution_bitcast_fusion.2
  364.2 39.7 %all-reduce = (f32[16]{0:T(128)S(1)}, f32[16]{0:T(128)S(1)}, f32[16]{0:T(128)S(1)}) all-reduce(f32[16]{0:T(128)S(1)} %convolution_bitcast_fusion.2, f32[16]{0:T(128)S(1)} %convolution_bitcast_fusion.1, f32[16]{0:T(128)S(1)} %convolution_bitcast_fusion), channel_id=1, replica_groups=mesh['dp'=16,'tensor'=2] {'dp','tensor'}, use_global_device_ids=true, to_apply=%region_11.12 | all-reduce | flops 48 | bytes 384 | tf_op jit(solution)/shard_map/psum | solution.py:53
  403.9 0.7 dynamic_slice.31
  404.6 0.6 dynamic_slice.30
  405.2 0.6 dynamic_slice.29
  (16 shorter events, 0.1 us)
Async XLA Ops:
  7.2 38.3 %all-gather.3.cloned.1.call-start = ((), (), s32[]{:S(2)}) async-start(), calls=%async_computation | async-start | bytes 3145728 | tf_op jit(solution)/shard_map/all_gather | solution.py:12
  7.9 296.1 %all-gather.5.cloned.1.call-start = ((), (), s32[]{:S(2)}) async-start(), calls=%async_computation.1 | async-start | bytes 55705600 | tf_op jit(solution)/shard_map/all_gather | solution.py:20
  47.5 297.3 %copy-start = (s32[512]{0:T(512)S(1)}, s32[512]{0:T(512)}, u32[]{:S(2)}) copy-start(s32[512]{0:T(512)} %param.10) | copy-start | bytes 6148
  339.9 23.5 %copy-start.3 = (s32[512]{0:T(512)S(1)}, s32[512]{0:T(512)}, u32[]{:S(2)}) copy-start(s32[512]{0:T(512)} %param.11) | copy-start | bytes 6148
  339.9 23.6 %copy-start.4 = (s32[16]{0:T(128)S(1)}, s32[16]{0:T(128)}, u32[]{:S(2)}) copy-start(s32[16]{0:T(128)} %param.13) | copy-start | bytes 196
  363.4 44.3 %copy-start.1 = (f32[256]{0:T(256)}, f32[256]{0:T(256)S(1)}, u32[]{:S(2)}) copy-start(f32[256]{0:T(256)S(1)} %get-tuple-element.13) | copy-start | bytes 3076
  364.0 43.8 %copy-start.2 = (f32[256]{0:T(256)}, f32[256]{0:T(256)S(1)}, u32[]{:S(2)}) copy-start(f32[256]{0:T(256)S(1)} %subtract_multiply_fusion.1) | copy-start | bytes 3076
Sparse Core Ops, SparseCore 0:
  9.5 35.8 all-gather.2
  47.0 256.9 all-gather.4
where the time goes:
time: 417 us
  waiting for transfers between devices  293 us (70%)
  blocking collectives  49.7 us (12%)
  matrix products  36.5 us (9%)
  between operations  18.3 us (4%)
  other arithmetic  16.7 us (4%)
    all_gather x1, waiting for transfers between devices, per_device(): piece = lax.all_gather(head_weight, 'dp', axis=1, tiled=True)  257 us
    psum x1, blocking collectives, per_device(): lax.psum((lp_part, ent_part, count_part), ('dp', 'tensor'))  39.7 us
    dot_general x1, matrix products, per_device(): logits = jnp.dot(normed, piece, preferred_element_type=jnp.float32)  35.8 us
    all_gather x1, waiting for transfers between devices, per_device(): whole = lax.all_gather(hidden_states, 'tensor', axis=1, tiled=True)  35.1 us
    reduce_sum x1, other arithmetic, per_device(): jnp.sum(expo * shifted, axis=1)  13.5 us
  transfers between devices with their start and end apart: 2, of which 2 were waited for; matrix products, arithmetic and copies ran while one was open for 1% of the time, Pallas kernels for 0%

commit v1 on v0

--- a/solution.py
+++ b/solution.py
@@ -6,10 +6,30 @@
 EPS = 1e-05
 
 
+def _balance_frames(piece_in, axis_no):
+    block_last = list(piece_in.shape[1:])
+    block_last[axis_no] *= piece_in.shape[0]
+    return jnp.moveaxis(piece_in, 0, axis_no).reshape(block_last)
+
+
+def types_fill(patch, named_axis):
+    amount_of = lax.axis_size(named_axis)
+    mid_arr = patch[None]
+    for p in range(amount_of.bit_length() - 1):
+        z = 1 << p
+        shaped = lax.ppermute(mid_arr, named_axis, tuple(((j0, j0 ^ z) for j0 in range(amount_of))))
+        value_now = jnp.stack([mid_arr, shaped], 0)
+        reached = lax.axis_index(named_axis)
+        found_now = reached >> p & 1
+        mid_arr = jnp.where(found_now == 0, value_now, value_now[::-1]).reshape(-1, *patch.shape)
+    return mid_arr
+
+
 def per_device(
     hidden_states, norm_gain, head_weight, target_ids, loss_mask, seq_lengths, slot_order
 ):
-    whole = lax.all_gather(hidden_states, "tensor", axis=1, tiled=True)
+    val2 = types_fill(hidden_states, "tensor")
+    whole = _balance_frames(val2, 1)
     values = whole.astype(jnp.float32)
     square = jnp.mean(values * values, axis=1, keepdims=True)
     normed = (values * lax.rsqrt(square + EPS) * norm_gain.astype(jnp.float32)).astype(jnp.bfloat16)

time: 417 us -> 382 us (0.916)
  waiting for transfers between devices: 293 us -> 255 us
    all_gather x1 -> x0, waiting for transfers between devices: 35.1 us -> none  [per_device(): whole = lax.all_gather(hidden_states, 'tensor', axis=1, tiled=True)]
    all_gather x1, waiting for transfers between devices: 257 us -> 232 us  [per_device(): piece = lax.all_gather(head_weight, 'dp', axis=1, tiled=True)]
    ppermute x0 -> x1, waiting for transfers between devices: none -> 22.8 us  [types_fill(): lax.ppermute(mid_arr, named_axis, tuple(((j0, j0 ^ z) for j0 in range(amo...]
where the time goes in v1:
time: 382 us; the launch traced here: 381 us
  waiting for transfers between devices  255 us (67%)
  blocking collectives  49.6 us (13%)
  matrix products  35.7 us (9%)
  between operations  18.4 us (5%)
  other arithmetic  15.8 us (4%)
    all_gather x1, waiting for transfers between devices, per_device(): piece = lax.all_gather(head_weight, 'dp', axis=1, tiled=True)  232 us
    psum x1, blocking collectives, per_device(): lax.psum((lp_part, ent_part, count_part), ('dp', 'tensor'))  39.7 us
    dot_general x1, matrix products, per_device(): logits = jnp.dot(normed, piece, preferred_element_type=jnp.float32)  35 us
    ppermute x1, waiting for transfers between devices, types_fill(): lax.ppermute(mid_arr, named_axis, tuple(((j0, j0 ^ z) for j0 in range(amo...  22.8 us
    reduce_sum x1, other arithmetic, per_device(): jnp.sum(expo * shifted, axis=1)  13.5 us
  transfers between devices with their start and end apart: 2, of which 2 were waited for; matrix products, arithmetic and copies ran while one was open for 1% of the time, Pallas kernels for 0%

profile of v1, /device:TPU:0, one launch (start us, length us, event | category | flops | bytes accessed | tf_op | source)
XLA Modules:
  0.0 381.3 jit_solution(14312540675489571394)
XLA Ops:
  7.2 0.7 all-gather.2.cloned.1.call-update
  7.9 1.5 copy.15
  9.4 3.0 collective-permute-start
  12.4 0.1 copy.17
  12.6 0.1 reduce.3
  12.7 0.1 convert_reduce_fusion
  12.8 22.8 %collective-permute-done = bf16[1,512,1024]{1,2,0:T(8,128)(2,1)S(1)} collective-permute-done((bf16[1,512,1024]{1,2,0:T(8,128)(2,1)S(1)}, bf16[1,512,1024]{1,2,0:T(8,128)(2,1)S(1)}, u32[]{:S(2)}, u32[]{:S(2)}) %collective-permute-start) | collective-permute-done | bytes 1048608 | tf_op jit(solution)/shard_map/ppermute | solution.py:20
  35.6 0.2 pad_maximum_fusion
  35.8 0.6 multiply_reduce_fusion
  36.4 0.6 fusion.3
  37.0 0.4 fusion.2
  37.5 231.9 %all-gather.2.cloned.1.call-done = bf16[2048,12800]{0,1:T(8,128)(2,1)} async-done(((bf16[2048,800]{0,1:T(8,128)(2,1)}), bf16[2048,12800]{0,1:T(8,128)(2,1)}) %all-gather.2.cloned.1.call-update) | async-done | bytes 52428816 | tf_op jit(solution)/shard_map/all_gather | solution.py:40
  269.3 35.0 %fusion.13 = (f32[512]{0:T(512)S(1)}, f32[512,12800]{1,0:T(8,128)}) fusion(bf16[512,2048]{0,1:T(8,128)(2,1)S(1)} %fusion.2, bf16[2048,12800]{0,1:T(8,128)(2,1)} %all-gather.2.cloned.1.call-done), kind=kOutput, calls=%fused_computation.33 | convolution fusion | flops 26850099200 | bytes 80742400 | tf_op jit(solution)/shard_map/dot_general | solution.py:43
  304.3 4.9 %pmax.7 = f32[512]{0:T(512)S(1)} all-reduce(f32[512]{0:T(512)S(1)} %broadcast_maximum_fusion), channel_id=1, replica_groups=mesh['dp'=16,'tensor'=2] {'tensor'}, use_global_device_ids=true, to_apply=%region_4.5 | all-reduce | flops 512 | bytes 4096 | tf_op jit(solution)/shard_map/pmax | solution.py:53
  309.3 13.5 %fusion = (f32[512]{0:T(512)S(1)}, f32[512]{0:T(512)S(1)}, f32[512]{0:T(512)S(1)}) fusion(f32[512,12800]{1,0:T(8,128)} %get-tuple-element.18, f32[512]{0:T(512)S(1)} %broadcast_maximum_fusion, s32[512]{0:T(512)S(1)} %copy-done.1, s32[12800]{0:T(1024)S(1)} %iota_add_fusion), kind=kLoop, calls=%fused_computation.2 | loop fusion | flops 45873664 | bytes 26275840 | tf_op jit(solution)/shard_map/reduce_sum | solution.py:50
  322.8 5.0 %all-reduce.1 = (f32[512]{0:T(512)S(1)}, f32[512]{0:T(512)S(1)}, f32[512]{0:T(512)S(1)}) all-reduce(f32[512]{0:T(512)S(1)} %get-tuple-element.6, f32[512]{0:T(512)S(1)} %get-tuple-element.16, f32[512]{0:T(512)S(1)} %get-tuple-element.15), channel_id=1, replica_groups=mesh['dp'=16,'tensor'=2] {'tensor'}, use_global_device_ids=true, to_apply=%region_2.3 | all-reduce | flops 1536 | bytes 12288 | tf_op jit(solution)/shard_map/psum | solution.py:55
  327.9 0.2 convolution_bitcast_fusion
  328.1 0.2 convolution_bitcast_fusion.1
  328.4 0.1 subtract_multiply_fusion.1
  328.4 0.2 convolution_bitcast_fusion.2
  328.7 39.7 %all-reduce = (f32[16]{0:T(128)S(1)}, f32[16]{0:T(128)S(1)}, f32[16]{0:T(128)S(1)}) all-reduce(f32[16]{0:T(128)S(1)} %convolution_bitcast_fusion.2, f32[16]{0:T(128)S(1)} %convolution_bitcast_fusion.1, f32[16]{0:T(128)S(1)} %convolution_bitcast_fusion), channel_id=1, replica_groups=mesh['dp'=16,'tensor'=2] {'dp','tensor'}, use_global_device_ids=true, to_apply=%region_11.12 | all-reduce | flops 48 | bytes 384 | tf_op jit(solution)/shard_map/psum | solution.py:73
  368.4 0.7 dynamic_slice.31
  369.0 0.6 dynamic_slice.30
  369.6 0.6 dynamic_slice.29
  (23 shorter events, 0.2 us)
Async XLA Ops:
  7.2 5.3 %copy-start = (bf16[2048]{0:T(1024)(128)(2,1)S(1)}, bf16[2048]{0:T(1024)(128)(2,1)}, u32[]{:S(2)}) copy-start(bf16[2048]{0:T(1024)(128)(2,1)} %param.8) | copy-start | bytes 12292
  7.2 5.3 %copy-start.4 = (s32[16]{0:T(128)S(1)}, s32[16]{0:T(128)}, u32[]{:S(2)}) copy-start(s32[16]{0:T(128)} %param.12) | copy-start | bytes 196
  7.2 262.1 %all-gather.2.cloned.1.call-start = ((), (), s32[]{:S(2)}) async-start(), calls=%async_computation | async-start | bytes 55705600 | tf_op jit(solution)/shard_map/all_gather | solution.py:40
  9.4 26.2 %collective-permute-start = (bf16[1,512,1024]{1,2,0:T(8,128)(2,1)S(1)}, bf16[1,512,1024]{1,2,0:T(8,128)(2,1)S(1)}, u32[]{:S(2)}, u32[]{:S(2)}) collective-permute-start(bf16[1,512,1024]{1,2,0:T(8,128)(2,1)S(1)} %bitcast.28), channel_id=1, source_target_pairs={{0,1},{1,0},{2,3},{3,2},{4,5},{5,4},{6,7},{7,6},{8,9},{9,8},{10,11... | collective-permute-start | bytes 3145736 | tf_op jit(solution)/shard_map/ppermute | solution.py:20
  37.4 271.8 %copy-start.1 = (s32[512]{0:T(512)S(1)}, s32[512]{0:T(512)}, u32[]{:S(2)}) copy-start(s32[512]{0:T(512)} %param.10) | copy-start | bytes 6148
  309.3 18.5 %copy-start.5 = (s32[512]{0:T(512)S(1)}, s32[512]{0:T(512)}, u32[]{:S(2)}) copy-start(s32[512]{0:T(512)} %param.11) | copy-start | bytes 6148
  309.3 18.6 %copy-start.6 = (s32[16]{0:T(128)S(1)}, s32[16]{0:T(128)}, u32[]{:S(2)}) copy-start(s32[16]{0:T(128)} %param.13) | copy-start | bytes 196
  327.9 44.3 %copy-start.2 = (f32[256]{0:T(256)}, f32[256]{0:T(256)S(1)}, u32[]{:S(2)}) copy-start(f32[256]{0:T(256)S(1)} %get-tuple-element.13) | copy-start | bytes 3076
  328.4 43.8 %copy-start.3 = (f32[256]{0:T(256)}, f32[256]{0:T(256)S(1)}, u32[]{:S(2)}) copy-start(f32[256]{0:T(256)S(1)} %subtract_multiply_fusion.1) | copy-start | bytes 3076
Sparse Core Ops, SparseCore 0:
  9.6 259.6 all-gather.1
